TPU v7x, 768 devices: a whole 4x8x12 slice. The times are simulated.
768 devices in a mesh: row: 64 (over y, x, z_hi), col: 12 (over z_lo, core).
Axes of the slice: x: 4, y: 8, z: 12 (z_hi: 2, z_lo: 6; z = z_hi * 6 + z_lo), core: 2. Of those that a mesh axis runs over, the one named last changes fastest.
Arguments:
- node_features: bfloat16 [98304, 128], P(('row', 'col')), may hold values from -6 to 6
- weight: bfloat16 [128, 256], replicated, may hold values from -0.5 to 0.5
- block_values: bfloat16 [64, 12, 72, 128, 128], P('row', 'col'), may hold values from -0.21875 to 0.21875
- tile_rows: int32 [64, 12, 72], P('row', 'col'), may hold values from 0 to 11, as said below
- tile_cols: int32 [64, 12, 72], P('row', 'col'), may hold values from 0 to 63
- tile_count: int32 [64, 12], P('row', 'col'), may hold values from 18 to 72, as said below
- grad_out: bfloat16 [98304, 256], P(('row', 'col')), may hold values from -6 to 6
Outputs:
- activations: bfloat16 [98304, 256], P(('row', 'col'))
- grad_features: bfloat16 [98304, 128], P(('row', 'col'))
Inputs may be any that keep to these rules, and one draw needn't show every extreme that they name: In each tile, the slots below tile_count name distinct pairs (tile_rows, tile_cols); later slots are not part of A. `tile_count`: some tile holds 72 used slots in every draw.
All inputs are finite; a program needn't handle non-finite values.
Results may differ from a plain program's by a relative error of at most 0.018.
Values may be sent and summed in bfloat16 or wider, within the bound.
No kernel may reach another device: no remote copies, remote signals or barrier semaphores. Data moves between devices by JAX's collectives and lax.ppermute only.
A program may use at most 64 MiB of HBM per device.

v0:
```python
import jax
import jax.numpy as jnp
from jax import lax
from jax.sharding import PartitionSpec as P


def tile_forward(values, row_ids, col_ids, tile_total, source, row_blocks):
    slots = values.shape[0]
    block_size = values.shape[1]
    feat_width = source.shape[-1]
    picked = jnp.take(source.reshape(-1, block_size, feat_width), col_ids, axis=0)
    product = jnp.einsum("bik,bkf->bif", values, picked, preferred_element_type=jnp.float32)
    live_slot = jnp.arange(slots, dtype=jnp.int32) < tile_total
    select = (
        (row_ids[None, :] == jnp.arange(row_blocks, dtype=jnp.int32)[:, None]) & live_slot[None, :]
    ).astype(jnp.float32)
    summed = jnp.einsum("rb,bif->rif", select, product, precision=lax.Precision.HIGHEST)
    return summed.reshape(row_blocks * block_size, feat_width)


def per_device(node_features, weight, block_values, tile_rows, tile_cols, tile_count, grad_out):
    block_size = block_values.shape[-1]
    values = block_values.reshape(-1, block_size, block_size)
    row_ids = tile_rows.reshape(-1)
    col_ids = tile_cols.reshape(-1)
    tile_total = tile_count.reshape(())
    node_rows = node_features.shape[0]
    feat_in = node_features.shape[1]
    row_blocks = lax.axis_size("col") * node_rows // block_size
    transformed = jnp.dot(node_features, weight, preferred_element_type=jnp.float32).astype(
        jnp.bfloat16
    )
    columns = lax.all_gather(transformed, "row", axis=0, tiled=True)
    partial_value = tile_forward(values, row_ids, col_ids, tile_total, columns, row_blocks)
    pre = lax.psum_scatter(
        partial_value.astype(jnp.bfloat16), "col", scatter_dimension=0, tiled=True
    ).astype(jnp.float32)
    sigm = jax.nn.sigmoid(pre)
    activations = (pre * sigm).astype(jnp.bfloat16)
    pre_grad = (grad_out.astype(jnp.float32) * (sigm * (1.0 + pre * (1.0 - sigm)))).astype(
        jnp.bfloat16
    )
    back = jnp.dot(pre_grad, weight.T, preferred_element_type=jnp.float32).astype(jnp.bfloat16)
    rows_back = lax.all_gather(back, "col", axis=0, tiled=True)
    picked = jnp.take(rows_back.reshape(-1, block_size, feat_in), row_ids, axis=0)
    product = jnp.einsum("bki,bkf->bif", values, picked, preferred_element_type=jnp.float32)
    live_slot = jnp.arange(values.shape[0], dtype=jnp.int32) < tile_total
    select = (
        (
            col_ids[None, :]
            == jnp.arange(lax.axis_size("row") * node_rows // block_size, dtype=jnp.int32)[:, None]
        )
        & live_slot[None, :]
    ).astype(jnp.float32)
    summed = jnp.einsum("cb,bif->cif", select, product, precision=lax.Precision.HIGHEST)
    grad_sum = lax.psum_scatter(
        summed.reshape(lax.axis_size("row") * node_rows, feat_in),
        "row",
        scatter_dimension=0,
        tiled=True,
    )
    return (activations, grad_sum.astype(jnp.bfloat16))


def solution(mesh):
    placed = (
        P(("row", "col"), None),
        P(),
        P("row", "col", None, None, None),
        P("row", "col", None),
        P("row", "col", None),
        P("row", "col"),
        P(("row", "col"), None),
    )
    return jax.shard_map(
        per_device,
        mesh=mesh,
        in_specs=placed,
        out_specs=(P(("row", "col"), None), P(("row", "col"), None)),
        check_vma=False,
    )
```

profile of v0, /device:TPU:96, one launch (start us, length us, event | category | flops | bytes accessed | tf_op | source)
XLA Modules:
  0.0 972.8 jit_solution(8115529835465399301)
XLA Ops:
  7.2 0.0 all-gather.2.cloned.1.call-start
  7.2 1.8 convolution_convert_fusion
  9.0 0.0 reduce-scatter.3.cloned.1.call-start
  9.7 0.7 fusion.36
  10.4 0.7 compare_and_fusion.1
  11.1 193.9 %all-gather.2.cloned.1.call-done = bf16[8192,256]{1,0:T(8,128)(2,1)} async-done(((bf16[128,256]{1,0:T(8,128)(2,1)}), bf16[8192,256]{1,0:T(8,128)(2,1)}) %all-gather.2.cloned.1.call-update) | async-done | bytes 4194320 | tf_op jit(solution)/shard_map/all_gather | solution.py:33
  205.0 7.8 gather_fusion
  212.7 7.5 fusion.4
  220.2 9.7 %copy.11 = f32[72,256,128]{1,0,2:T(8,128)} copy(f32[72,256,128]{2,1,0:T(8,128)} %fusion.4) | data formatting | bytes 18874368 | tf_op jit(solution)/shard_map/bik,bkf->bif/dot_general | solution.py:12
  230.0 7.0 fusion.13
  236.9 1.1 copy.9
  238.1 0.0 reduce-scatter.5.cloned.1.call-start
  238.2 61.6 %reduce-scatter.3.cloned.1.call-done = bf16[128,256]{1,0:T(8,128)(2,1)} async-done(((bf16[1536,256]{1,0:T(8,128)(2,1)}), bf16[128,256]{1,0:T(8,128)(2,1)}) %reduce-scatter.3.cloned.1.call-update) | async-done | bytes 65552 | tf_op jit(solution)/shard_map/reduce_scatter | solution.py:35
  299.8 1.0 convolution_convert_fusion.1
  300.8 22.6 %all_gather.7 = bf16[1536,128]{1,0:T(8,128)(2,1)S(1)} all-gather(bf16[128,128]{1,0:T(8,128)(2,1)S(1)} %convolution_convert_fusion.1), channel_id=1, replica_groups=mesh['row'=64,'col'=12] {'col'}, dimensions={0}, use_global_device_ids=true | all-gather | bytes 425984 | tf_op jit(solution)/shard_map/all_gather | solution.py:44
  323.4 2.5 gather_fusion.1
  325.8 4.8 fusion.7
  330.6 6.1 copy.12
  336.7 4.9 fusion.2
  341.6 4.4 copy.10
  346.0 0.8 copy-done.2
  346.8 0.7 fusion.20
  347.5 617.4 %reduce-scatter.5.cloned.1.call-done = f32[128,128]{1,0:T(8,128)} async-done(((f32[8192,128]{1,0:T(8,128)}), f32[128,128]{1,0:T(8,128)}) %reduce-scatter.5.cloned.1.call-update) | async-done | bytes 65552 | tf_op jit(solution)/shard_map/reduce_scatter | solution.py:56
  964.9 1.5 convert_element_type.37
  (19 shorter events, 0.1 us)
Async XLA Ops:
  7.2 205.6 %copy-start = (bf16[1,1,72,128,128]{4,3,2,1,0:T(8,128)(2,1)S(1)}, bf16[1,1,72,128,128]{4,3,2,1,0:T(8,128)(2,1)}, u32[]{:S(2)}) copy-start(bf16[1,1,72,128,128]{4,3,2,1,0:T(8,128)(2,1)} %param.9) | copy-start | bytes 7077892
  7.2 197.8 %all-gather.2.cloned.1.call-start = ((), (), s32[]{:S(2)}) async-start(), calls=%async_computation.2 | async-start | bytes 4259840 | tf_op jit(solution)/shard_map/all_gather | solution.py:33
  9.0 290.7 %reduce-scatter.3.cloned.1.call-start = ((), (), s32[]{:S(2)}) async-start(), calls=%async_computation.3 | async-start | bytes 851968 | tf_op jit(solution)/shard_map/reduce_scatter | solution.py:35
  220.2 9.7 %copy-start.3 = (s32[1,1,72]{2,1,0:T(1,128)S(1)}, s32[1,1,72]{2,1,0:T(1,128)}, u32[]{:S(2)}) copy-start(s32[1,1,72]{2,1,0:T(1,128)} %param.10) | copy-start | bytes 868
  230.0 69.8 %copy-start.1 = (bf16[128,256]{1,0:T(8,128)(2,1)S(1)}, bf16[128,256]{1,0:T(8,128)(2,1)}, u32[]{:S(2)}) copy-start(bf16[128,256]{1,0:T(8,128)(2,1)} %param.8) | copy-start | bytes 196612
  230.0 69.8 %copy-start.5 = (bf16[128,256]{1,0:T(8,128)(2,1)S(1)}, bf16[128,256]{1,0:T(8,128)(2,1)}, u32[]{:S(2)}) copy-start(bf16[128,256]{1,0:T(8,128)(2,1)} %param.13) | copy-start | bytes 196612
  238.1 726.7 %reduce-scatter.5.cloned.1.call-start = ((), (), s32[]{:S(2)}) async-start(), calls=%async_computation.4 | async-start | bytes 4259840 | tf_op jit(solution)/shard_map/reduce_scatter | solution.py:56
  330.6 6.1 copy-start.4
  346.0 0.8 copy-start.2
Sparse Core Ops, SparseCore 0:
  14.0 190.9 all-gather.1
  238.2 61.4 reduce-scatter.2
  346.1 618.6 reduce-scatter.4
where the time goes:
time: 973 us
  waiting for transfers between devices  873 us (90%)
  local copies, waits for them, and re-layouts  32.4 us (3%)
  matrix products  27 us (3%)
  blocking collectives  22.6 us (2%)
  between operations  14.5 us (1%)
    reduce_scatter x1, waiting for transfers between devices, per_device(): lax.psum_scatter(summed.reshape(lax.axis_size('row') * node_rows, feat_in...  617 us
    all_gather x1, waiting for transfers between devices, per_device(): columns = lax.all_gather(transformed, 'row', axis=0, tiled=True)  194 us
    reduce_scatter x1, waiting for transfers between devices, per_device(): lax.psum_scatter(partial_value.astype(jnp.bfloat16), 'col', scatter_dimen...  61.6 us
    all_gather x1, blocking collectives, per_device(): rows_back = lax.all_gather(back, 'col', axis=0, tiled=True)  22.6 us
  transfers between devices with their start and end apart: 3, of which 3 were waited for; matrix products, arithmetic and copies ran while one was open for 0% of the time, Pallas kernels for 0%

commit v1 on v0

v1 whole, which is shorter than its diff:
```python
import jax
import jax.numpy as jnp
from jax import lax
from jax.sharding import Mesh
from jax.sharding import PartitionSpec as P

PHYS = (("y", 8), ("x", 4), ("zh", 2), ("zl", 6), ("core", 2))
ALL = tuple(name for name, _ in PHYS)
ROW = ("y", "x", "zh")
COL = ("zl", "core")
XY = ("y", "x")


def tile_forward(values, row_ids, col_ids, tile_total, source, row_blocks):
    slots = values.shape[0]
    block_size = values.shape[1]
    feat_width = source.shape[-1]
    picked = jnp.take(source.reshape(-1, block_size, feat_width), col_ids, axis=0)
    product = jnp.einsum("bik,bkf->bif", values, picked, preferred_element_type=jnp.float32)
    live_slot = jnp.arange(slots, dtype=jnp.int32) < tile_total
    select = (
        (row_ids[None, :] == jnp.arange(row_blocks, dtype=jnp.int32)[:, None]) & live_slot[None, :]
    ).astype(jnp.float32)
    summed = jnp.einsum("rb,bif->rif", select, product, precision=lax.Precision.HIGHEST)
    return summed.reshape(row_blocks * block_size, feat_width)


def gather_columns(x):
    pair = lax.all_gather(x, "zh", axis=0, tiled=True)
    peers = lax.axis_size(XY)
    spread = jnp.broadcast_to(pair[None], (peers,) + pair.shape)
    return lax.all_to_all(spread, XY, 0, 0, tiled=False).reshape(-1, x.shape[1])


def scatter_rows(total, zh):
    peers = lax.axis_size(XY)
    parts = total.astype(jnp.bfloat16).reshape(peers, -1, total.shape[1])
    got = lax.all_to_all(parts, XY, 0, 0, tiled=False).astype(jnp.float32).sum(0)
    halves = got.reshape(2, -1, total.shape[1])
    mine = lax.dynamic_index_in_dim(halves, zh, 0, keepdims=False)
    other = lax.dynamic_index_in_dim(halves, 1 - zh, 0, keepdims=False)
    return mine + lax.ppermute(other, "zh", [(0, 1), (1, 0)])


def per_device(node_features, weight, block_values, tile_rows, tile_cols, tile_count, grad_out):
    block_size = block_values.shape[-1]
    values = block_values.reshape(-1, block_size, block_size)
    row_ids = tile_rows.reshape(-1)
    col_ids = tile_cols.reshape(-1)
    tile_total = tile_count.reshape(())
    node_rows = node_features.shape[0]
    feat_in = node_features.shape[1]
    n_col = lax.axis_size(COL)
    n_row = lax.axis_size(ROW)
    row_blocks = n_col * node_rows // block_size
    zh = lax.axis_index("zh")

    features = gather_columns(node_features)
    columns = jnp.dot(features, weight, preferred_element_type=jnp.float32).astype(jnp.bfloat16)
    partial_value = tile_forward(values, row_ids, col_ids, tile_total, columns, row_blocks)
    pieces = partial_value.astype(jnp.bfloat16).reshape(n_col, node_rows, -1)
    pre = lax.all_to_all(pieces, COL, 0, 0, tiled=False).astype(jnp.float32).sum(0)
    sigm = jax.nn.sigmoid(pre)
    activations = (pre * sigm).astype(jnp.bfloat16)
    pre_grad = (grad_out.astype(jnp.float32) * (sigm * (1.0 + pre * (1.0 - sigm)))).astype(
        jnp.bfloat16
    )
    back = jnp.dot(pre_grad, weight.T, preferred_element_type=jnp.float32).astype(jnp.bfloat16)
    rows_back = lax.all_gather(back, COL, axis=0, tiled=True)
    picked = jnp.take(rows_back.reshape(-1, block_size, feat_in), row_ids, axis=0)
    product = jnp.einsum("bki,bkf->bif", values, picked, preferred_element_type=jnp.float32)
    live_slot = jnp.arange(values.shape[0], dtype=jnp.int32) < tile_total
    select = (
        (
            col_ids[None, :]
            == jnp.arange(n_row * node_rows // block_size, dtype=jnp.int32)[:, None]
        )
        & live_slot[None, :]
    ).astype(jnp.float32)
    summed = jnp.einsum("cb,bif->cif", select, product, precision=lax.Precision.HIGHEST)
    grad_sum = scatter_rows(summed.reshape(n_row * node_rows, feat_in), zh)
    return (activations, grad_sum.astype(jnp.bfloat16))


def solution(mesh):
    sizes = tuple(size for _, size in PHYS)
    fine = Mesh(mesh.devices.reshape(sizes), ALL)
    placed = (
        P(ALL, None),
        P(),
        P(ROW, COL, None, None, None),
        P(ROW, COL, None),
        P(ROW, COL, None),
        P(ROW, COL),
        P(ALL, None),
    )
    return jax.shard_map(
        per_device,
        mesh=fine,
        in_specs=placed,
        out_specs=(P(ALL, None), P(ALL, None)),
        check_vma=False,
    )
```

time: 973 us -> 270 us (0.28)
  the two profiles are of different devices: /device:TPU:96 before, /device:TPU:16 now
where the time goes in v1:
time: 270 us; the launch traced here: 269 us
  waiting for transfers between devices  131 us (49%)
  blocking collectives  37.7 us (14%)
  starting transfers between devices  34.3 us (13%)
  local copies, waits for them, and re-layouts  31.7 us (12%)
  matrix products  29.2 us (11%)
  other arithmetic  3.33 us (1%)
    all_to_all x1, waiting for transfers between devices, scatter_rows(): lax.all_to_all(parts, XY, 0, 0, tiled=False).astype(jnp.float32).sum(0)  50.7 us
    all_to_all x1, waiting for transfers between devices, gather_columns(): return lax.all_to_all(spread, XY, 0, 0, tiled=False).reshape(-1, x.shape[1])  48.7 us
    all_to_all x1, waiting for transfers between devices, per_device(): lax.all_to_all(pieces, COL, 0, 0, tiled=False).astype(jnp.float32).sum(0)  30.3 us
    all_gather x1, blocking collectives, per_device(): rows_back = lax.all_gather(back, COL, axis=0, tiled=True)  21.5 us
    all_gather x1, blocking collectives, gather_columns(): pair = lax.all_gather(x, 'zh', axis=0, tiled=True)  16.2 us
    all_to_all x1, starting transfers between devices, gather_columns(): return lax.all_to_all(spread, XY, 0, 0, tiled=False).reshape(-1, x.shape[1])  10.2 us
    ppermute x1, starting transfers between devices, scatter_rows(): return mine + lax.ppermute(other, 'zh', [(0, 1), (1, 0)])  10.2 us
    dot_general x1, local copies, waits for them, and re-layouts, tile_forward(): jnp.einsum('bik,bkf->bif', values, picked, preferred_element_type=jnp.flo...  9.67 us
  transfers between devices with their start and end apart: 4, of which 4 were waited for; matrix products, arithmetic and copies ran while one was open for 0% of the time, Pallas kernels for 0%

profile of v1, /device:TPU:16, one launch (start us, length us, event | category | flops | bytes accessed | tf_op | source)
XLA Modules:
  0.0 268.9 jit_solution(1577200145339025007)
XLA Ops:
  0.6 16.2 %all_gather.6 = bf16[256,128]{1,0:T(8,128)(2,1)S(1)} all-gather(bf16[128,128]{1,0:T(8,128)(2,1)} %param.7), channel_id=1, replica_groups=mesh['y'=8,'x'=4,'zh'=2,'zl'=6,'core'=2] {'zh'}, dimensions={0}, use_global_device_ids=true | all-gather | bytes 98304 | tf_op jit(solution)/shard_map/all_gather | solution.py:29
  16.8 1.8 broadcast_in_dim.31
  18.7 10.2 %all-to-all-start = ((bf16[32,256,128]{2,1,0:T(8,128)(2,1)}), bf16[32,256,128]{2,1,0:T(8,128)(2,1)}, u32[]{:S(2)}, u32[]{:S(2)}) async-start(bf16[32,256,128]{2,1,0:T(8,128)(2,1)} %broadcast_in_dim.31), calls=%async_computation | async-start | bytes 4194304 | tf_op jit(solution)/shard_map/all_to_all | solution.py:32
  29.6 48.7 %all-to-all-done = bf16[32,256,128]{2,1,0:T(8,128)(2,1)} async-done(((bf16[32,256,128]{2,1,0:T(8,128)(2,1)}), bf16[32,256,128]{2,1,0:T(8,128)(2,1)}, u32[]{:S(2)}, u32[]{:S(2)}) %all-to-all-start) | async-done | bytes 2097184 | tf_op jit(solution)/shard_map/all_to_all | solution.py:32
  78.3 4.8 %convolution_convert_fusion = bf16[8192,256]{1,0:T(8,128)(2,1)} fusion(bf16[8192,128]{1,0:T(8,128)(2,1)} %bitcast.4, bf16[128,256]{1,0:T(8,128)(2,1)S(1)} %copy-done.1), kind=kOutput, calls=%fused_computation.2 | convolution fusion | flops 538968064 | bytes 6356992 | tf_op jit(solution)/shard_map/dot_general | solution.py:59
  83.1 7.8 %gather_fusion = bf16[72,128,256]{2,1,0:T(8,128)(2,1)} fusion(bf16[64,128,256]{2,1,0:T(8,128)(2,1)} %bitcast.47, s32[1024]{0:T(1024)S(1)} %pad_clamp_fusion.1), kind=kCustom, calls=%fused_computation | custom fusion | bytes 9437472 | tf_op jit(solution)/shard_map/jit(_take)/gather | solution.py:18
  90.8 7.5 %fusion.3 = f32[72,128,256]{1,2,0:T(8,128)} fusion(bf16[72,128,256]{2,1,0:T(8,128)(2,1)} %gather_fusion, pred[72]{0:T(512)(128)(4,1)S(1)} %compare_and_fusion.1, bf16[1,1,72,128,128]{4,3,2,1,0:T(8,128)(2,1)S(1)} %copy-done), kind=kOutput, calls=%fused_computation.7 | convolution fusion | flops 606339072 | bytes 16515144 | tf_op jit(solution)/shard_map/bik,bkf->bif/dot_general | solution.py:19
  98.3 9.7 %copy.15 = f32[72,128,256]{2,0,1:T(8,128)} copy(f32[72,128,256]{1,2,0:T(8,128)} %fusion.3) | data formatting | bytes 18874368 | tf_op jit(solution)/shard_map/bik,bkf->bif/dot_general | solution.py:19
  108.0 6.9 %convolution_convert_fusion.2 = bf16[12,128,256]{2,0,1:T(8,128)(2,1)S(1)} fusion(f32[72,128,256]{2,0,1:T(8,128)} %copy.15, s32[72]{0:T(128)S(1)} %bitcast.52, pred[72]{0:T(512)(128)(4,1)S(1)} %iota_compare_fusion.2), kind=kOutput, calls=%fused_computation.17 | convolution fusion | flops 340133568 | bytes 10223976 | tf_op jit(solution)/shard_map/rb,bif->rif/dot_general | solution.py:24
  115.0 1.2 copy.16
  116.1 7.9 %all-to-all-start.1 = ((bf16[12,128,256]{2,1,0:T(8,128)(2,1)}), bf16[12,128,256]{2,1,0:T(8,128)(2,1)S(1)}, u32[]{:S(2)}, u32[]{:S(2)}) async-start(bf16[12,128,256]{2,1,0:T(8,128)(2,1)} %copy.16), calls=%async_computation.1 | async-start | bytes 1572864 | tf_op jit(solution)/shard_map/all_to_all | solution.py:62
  124.0 30.3 %all-to-all-done.1 = bf16[12,128,256]{2,1,0:T(8,128)(2,1)S(1)} async-done(((bf16[12,128,256]{2,1,0:T(8,128)(2,1)}), bf16[12,128,256]{2,1,0:T(8,128)(2,1)S(1)}, u32[]{:S(2)}, u32[]{:S(2)}) %all-to-all-start.1) | async-done | bytes 786464 | tf_op jit(solution)/shard_map/all_to_all | solution.py:62
  154.6 21.5 %all_gather.7 = bf16[1536,128]{1,0:T(8,128)(2,1)S(1)} all-gather(bf16[128,128]{1,0:T(8,128)(2,1)S(1)} %convolution_convert_fusion.3), channel_id=1, replica_groups=mesh['y'=8,'x'=4,'zh'=2,'zl'=6,'core'=2] {'zl','core'}, dimensions={0}, use_global_device_ids=true | all-gather | bytes 425984 | tf_op jit(solution)/shard_map/all_gather | solution.py:69
  176.1 2.5 gather_fusion.1
  178.6 4.8 %fusion.12 = f32[72,128,128]{1,2,0:T(8,128)} fusion(bf16[1,1,72,128,128]{4,3,2,1,0:T(8,128)(2,1)S(1)} %copy-done, bf16[72,128,128]{2,1,0:T(8,128)(2,1)} %gather_fusion.1, pred[72]{0:T(512)(128)(4,1)S(1)} %compare_and_fusion), kind=kOutput, calls=%fused_computation.14 | convolution fusion | flops 303169536 | bytes 9437256 | tf_op jit(solution)/shard_map/bki,bkf->bif/dot_general | solution.py:71
  183.4 6.1 %copy.18 = f32[72,128,128]{2,0,1:T(8,128)} copy(f32[72,128,128]{1,2,0:T(8,128)} %fusion.12) | data formatting | bytes 9437184 | tf_op jit(solution)/shard_map/bki,bkf->bif/dot_general | solution.py:71
  189.4 5.0 %convolution_convert_fusion.1 = bf16[64,128,128]{2,0,1:T(8,128)(2,1)S(1)} fusion(f32[72,128,128]{2,0,1:T(8,128)} %copy.18, s32[72]{0:T(128)S(1)} %bitcast.53, pred[72]{0:T(512)(128)(4,1)S(1)} %iota_compare_fusion.2), kind=kOutput, calls=%fused_computation.15 | convolution fusion | flops 907027456 | bytes 6816104 | tf_op jit(solution)/shard_map/cb,bif->cif/dot_general | solution.py:80
  194.5 2.7 copy.19
  197.1 6.0 %all-to-all-start.2 = ((bf16[32,256,128]{2,1,0:T(8,128)(2,1)}), bf16[32,256,128]{2,1,0:T(8,128)(2,1)}, u32[]{:S(2)}, u32[]{:S(2)}) async-start(bf16[32,256,128]{2,1,0:T(8,128)(2,1)} %bitcast.49), calls=%async_computation.2 | async-start | bytes 4194304 | tf_op jit(solution)/shard_map/all_to_all | solution.py:38
  203.1 50.7 %all-to-all-done.2 = bf16[32,256,128]{2,1,0:T(8,128)(2,1)} async-done(((bf16[32,256,128]{2,1,0:T(8,128)(2,1)}), bf16[32,256,128]{2,1,0:T(8,128)(2,1)}, u32[]{:S(2)}, u32[]{:S(2)}) %all-to-all-start.2) | async-done | bytes 2097184 | tf_op jit(solution)/shard_map/all_to_all | solution.py:38
  253.9 1.9 convert_reduce_fusion
  255.8 10.2 %collective-permute-start = (f32[128,128]{1,0:T(8,128)S(1)}, f32[128,128]{1,0:T(8,128)S(1)}, u32[]{:S(2)}, u32[]{:S(2)}) collective-permute-start(f32[128,128]{1,0:T(8,128)S(1)} %dynamic-slice_bitcast_fusion), channel_id=1, source_target_pairs={{0,12},{12,0},{1,13},{13,1},{2,14},{14,2},{3,15},{15,3},{4,16},{16... | collective-permute-start | bytes 196616 | tf_op jit(solution)/shard_map/ppermute | solution.py:42
  266.0 0.7 multiply_convert_fusion.1
  266.6 1.6 collective-permute-done
  (21 shorter events, 1.0 us)
Async XLA Ops:
  0.6 90.2 %copy-start = (bf16[1,1,72,128,128]{4,3,2,1,0:T(8,128)(2,1)S(1)}, bf16[1,1,72,128,128]{4,3,2,1,0:T(8,128)(2,1)}, u32[]{:S(2)}) copy-start(bf16[1,1,72,128,128]{4,3,2,1,0:T(8,128)(2,1)} %param.9) | copy-start | bytes 7077892
  18.7 10.9 %copy-start.3 = (s32[1,1,72]{2,1,0:T(1,128)S(1)}, s32[1,1,72]{2,1,0:T(1,128)}, u32[]{:S(2)}) copy-start(s32[1,1,72]{2,1,0:T(1,128)} %param.11) | copy-start | bytes 868
  18.7 59.6 %copy-start.1 = (bf16[128,256]{1,0:T(8,128)(2,1)S(1)}, bf16[128,256]{1,0:T(8,128)(2,1)}, u32[]{:S(2)}) copy-start(bf16[128,256]{1,0:T(8,128)(2,1)} %param.8) | copy-start | bytes 196612
  18.7 59.6 %all-to-all-start = ((bf16[32,256,128]{2,1,0:T(8,128)(2,1)}), bf16[32,256,128]{2,1,0:T(8,128)(2,1)}, u32[]{:S(2)}, u32[]{:S(2)}) async-start(bf16[32,256,128]{2,1,0:T(8,128)(2,1)} %broadcast_in_dim.31), calls=%async_computation | async-start | bytes 4194304 | tf_op jit(solution)/shard_map/all_to_all | solution.py:32
  98.3 9.7 %copy-start.2 = (s32[1,1,72]{2,1,0:T(1,128)S(1)}, s32[1,1,72]{2,1,0:T(1,128)}, u32[]{:S(2)}) copy-start(s32[1,1,72]{2,1,0:T(1,128)} %param.10) | copy-start | bytes 868
  114.9 39.5 %copy-start.4 = (bf16[128,256]{1,0:T(8,128)(2,1)S(1)}, bf16[128,256]{1,0:T(8,128)(2,1)}, u32[]{:S(2)}) copy-start(bf16[128,256]{1,0:T(8,128)(2,1)} %param.13) | copy-start | bytes 196612
  116.1 38.2 %all-to-all-start.1 = ((bf16[12,128,256]{2,1,0:T(8,128)(2,1)}), bf16[12,128,256]{2,1,0:T(8,128)(2,1)S(1)}, u32[]{:S(2)}, u32[]{:S(2)}) async-start(bf16[12,128,256]{2,1,0:T(8,128)(2,1)} %copy.16), calls=%async_computation.1 | async-start | bytes 1572864 | tf_op jit(solution)/shard_map/all_to_all | solution.py:62
  197.1 56.7 %all-to-all-start.2 = ((bf16[32,256,128]{2,1,0:T(8,128)(2,1)}), bf16[32,256,128]{2,1,0:T(8,128)(2,1)}, u32[]{:S(2)}, u32[]{:S(2)}) async-start(bf16[32,256,128]{2,1,0:T(8,128)(2,1)} %bitcast.49), calls=%async_computation.2 | async-start | bytes 4194304 | tf_op jit(solution)/shard_map/all_to_all | solution.py:38
  255.8 12.5 %collective-permute-start = (f32[128,128]{1,0:T(8,128)S(1)}, f32[128,128]{1,0:T(8,128)S(1)}, u32[]{:S(2)}, u32[]{:S(2)}) collective-permute-start(f32[128,128]{1,0:T(8,128)S(1)} %dynamic-slice_bitcast_fusion), channel_id=1, source_target_pairs={{0,12},{12,0},{1,13},{13,1},{2,14},{14,2},{3,15},{15,3},{4,16},{16... | collective-permute-start | bytes 196616 | tf_op jit(solution)/shard_map/ppermute | solution.py:42

commit v2 on v1

v2 whole, which is shorter than its diff:
```python
import jax
import jax.numpy as jnp
from jax import lax
from jax.sharding import Mesh
from jax.sharding import PartitionSpec as P
from jax.experimental import pallas as pl
from jax.experimental.pallas import tpu as pltpu

PHYS = (("y", 8), ("x", 4), ("zh", 2), ("zl", 6), ("core", 2))
ALL = tuple(name for name, _ in PHYS)
ROW = ("y", "x", "zh")
COL = ("zl", "core")
XY = ("y", "x")


def spmm_forward_kernel(rows_ref, cols_ref, count_ref, feat_ref, w_ref, vals_ref, out_ref, acc_ref):
    block = vals_ref.shape[1]
    acc_ref[...] = jnp.zeros_like(acc_ref)
    last_row = acc_ref.shape[0] // block - 1
    last_col = feat_ref.shape[0] // block - 1

    def body(s, carry):
        @pl.when(s < count_ref[0])
        def _():
            c = jnp.minimum(jnp.maximum(cols_ref[s], 0), last_col)
            r = jnp.minimum(jnp.maximum(rows_ref[s], 0), last_row)
            feat = feat_ref[pl.ds(pl.multiple_of(c * block, block), block), :]
            source = jnp.dot(feat, w_ref[...], preferred_element_type=jnp.float32).astype(
                jnp.bfloat16
            )
            rows = pl.ds(pl.multiple_of(r * block, block), block)
            acc_ref[rows, :] += jnp.dot(vals_ref[s], source, preferred_element_type=jnp.float32)

        return carry

    lax.fori_loop(0, vals_ref.shape[0], body, 0)
    out_ref[...] = acc_ref[...].astype(out_ref.dtype)


def spmm_backward_kernel(rows_ref, cols_ref, count_ref, back_ref, vals_ref, out_ref, acc_ref):
    block = vals_ref.shape[1]
    acc_ref[...] = jnp.zeros_like(acc_ref)
    last_row = back_ref.shape[0] // block - 1
    last_col = acc_ref.shape[0] // block - 1

    def body(s, carry):
        @pl.when(s < count_ref[0])
        def _():
            c = jnp.minimum(jnp.maximum(cols_ref[s], 0), last_col)
            r = jnp.minimum(jnp.maximum(rows_ref[s], 0), last_row)
            source = back_ref[pl.ds(pl.multiple_of(r * block, block), block), :]
            part = lax.dot_general(
                vals_ref[s], source, (((0,), (0,)), ((), ())), preferred_element_type=jnp.float32
            )
            cols = pl.ds(pl.multiple_of(c * block, block), block)
            acc_ref[cols, :] += part

        return carry

    lax.fori_loop(0, vals_ref.shape[0], body, 0)
    out_ref[...] = acc_ref[...].astype(out_ref.dtype)


def _specs(n_smem, n_vmem):
    return [pl.BlockSpec(memory_space=pltpu.SMEM)] * n_smem + [
        pl.BlockSpec(memory_space=pltpu.VMEM)
    ] * n_vmem


def spmm_forward(row_ids, col_ids, count, features, weight, values, row_blocks, interpret=False):
    block = values.shape[1]
    width = weight.shape[1]
    slots = values.shape[0]
    flops = slots * 2 * block * (features.shape[1] + block) * width
    return pl.pallas_call(
        spmm_forward_kernel,
        out_shape=jax.ShapeDtypeStruct((row_blocks * block, width), jnp.bfloat16),
        in_specs=_specs(3, 3),
        out_specs=pl.BlockSpec(memory_space=pltpu.VMEM),
        scratch_shapes=[pltpu.VMEM((row_blocks * block, width), jnp.float32)],
        cost_estimate=pl.CostEstimate(
            flops=flops,
            transcendentals=0,
            bytes_accessed=values.size * 2 + features.size * 2 + row_blocks * block * width * 2,
        ),
        interpret=interpret,
    )(row_ids, col_ids, count, features, weight, values)


def spmm_backward(row_ids, col_ids, count, back, values, col_blocks, interpret=False):
    block = values.shape[1]
    width = back.shape[1]
    slots = values.shape[0]
    return pl.pallas_call(
        spmm_backward_kernel,
        out_shape=jax.ShapeDtypeStruct((col_blocks * block, width), jnp.bfloat16),
        in_specs=_specs(3, 2),
        out_specs=pl.BlockSpec(memory_space=pltpu.VMEM),
        scratch_shapes=[pltpu.VMEM((col_blocks * block, width), jnp.float32)],
        cost_estimate=pl.CostEstimate(
            flops=slots * 2 * block * block * width,
            transcendentals=0,
            bytes_accessed=values.size * 2 + back.size * 2 + col_blocks * block * width * 2,
        ),
        interpret=interpret,
    )(row_ids, col_ids, count, back, values)


def gather_columns(x):
    pair = lax.all_gather(x, "zh", axis=0, tiled=True)
    peers = lax.axis_size(XY)
    spread = jnp.broadcast_to(pair[None], (peers,) + pair.shape)
    return lax.all_to_all(spread, XY, 0, 0, tiled=False).reshape(-1, x.shape[1])


def scatter_rows(total, zh):
    peers = lax.axis_size(XY)
    parts = total.astype(jnp.bfloat16).reshape(peers, -1, total.shape[1])
    got = lax.all_to_all(parts, XY, 0, 0, tiled=False).astype(jnp.float32).sum(0)
    halves = got.reshape(2, -1, total.shape[1])
    mine = lax.dynamic_index_in_dim(halves, zh, 0, keepdims=False)
    other = lax.dynamic_index_in_dim(halves, 1 - zh, 0, keepdims=False)
    return mine + lax.ppermute(other, "zh", [(0, 1), (1, 0)])


def per_device(node_features, weight, block_values, tile_rows, tile_cols, tile_count, grad_out):
    block_size = block_values.shape[-1]
    values = block_values.reshape(-1, block_size, block_size)
    row_ids = tile_rows.reshape(-1)
    col_ids = tile_cols.reshape(-1)
    node_rows = node_features.shape[0]
    n_col = lax.axis_size(COL)
    n_row = lax.axis_size(ROW)
    row_blocks = n_col * node_rows // block_size
    zh = lax.axis_index("zh")

    count = tile_count.reshape(1)
    features = gather_columns(node_features)
    partial_value = spmm_forward(row_ids, col_ids, count, features, weight, values, row_blocks)
    pieces = partial_value.reshape(n_col, node_rows, -1)
    pre = lax.all_to_all(pieces, COL, 0, 0, tiled=False).astype(jnp.float32).sum(0)
    sigm = jax.nn.sigmoid(pre)
    activations = (pre * sigm).astype(jnp.bfloat16)
    pre_grad = (grad_out.astype(jnp.float32) * (sigm * (1.0 + pre * (1.0 - sigm)))).astype(
        jnp.bfloat16
    )
    back = jnp.dot(pre_grad, weight.T, preferred_element_type=jnp.float32).astype(jnp.bfloat16)
    rows_back = lax.all_gather(back, COL, axis=0, tiled=True)
    summed = spmm_backward(row_ids, col_ids, count, rows_back, values, n_row * node_rows // block_size)
    grad_sum = scatter_rows(summed, zh)
    return (activations, grad_sum.astype(jnp.bfloat16))


def solution(mesh):
    sizes = tuple(size for _, size in PHYS)
    fine = Mesh(mesh.devices.reshape(sizes), ALL)
    placed = (
        P(ALL, None),
        P(),
        P(ROW, COL, None, None, None),
        P(ROW, COL, None),
        P(ROW, COL, None),
        P(ROW, COL),
        P(ALL, None),
    )
    return jax.shard_map(
        per_device,
        mesh=fine,
        in_specs=placed,
        out_specs=(P(ALL, None), P(ALL, None)),
        check_vma=False,
    )
```

time: 270 us -> 253 us (0.937)
  the two profiles are of different devices: /device:TPU:16 before, /device:TPU:14 now
where the time goes in v2:
time: 253 us; the launch traced here: 252 us
  waiting for transfers between devices  101 us (40%)
  blocking collectives  76 us (30%)
  Pallas kernels  39.5 us (16%)
  starting transfers between devices  29.4 us (12%)
  local copies, waits for them, and re-layouts  3.17 us (1%)
    all_to_all x1, waiting for transfers between devices, scatter_rows(): lax.all_to_all(parts, XY, 0, 0, tiled=False).astype(jnp.float32).sum(0)  49.8 us
    all_to_all x1, waiting for transfers between devices, gather_columns(): return lax.all_to_all(spread, XY, 0, 0, tiled=False).reshape(-1, x.shape[1])  48.2 us
    all_to_all x1, blocking collectives, per_device(): lax.all_to_all(pieces, COL, 0, 0, tiled=False).astype(jnp.float32).sum(0)  37.5 us
    pallas_call x1, Pallas kernels, spmm_forward(): pl.pallas_call(spmm_forward_kernel, out_shape=jax.ShapeDtypeStruct((row_b...  23.7 us
    all_gather x1, blocking collectives, per_device(): rows_back = lax.all_gather(back, COL, axis=0, tiled=True)  22.5 us
    all_gather x1, blocking collectives, gather_columns(): pair = lax.all_gather(x, 'zh', axis=0, tiled=True)  16.1 us
    pallas_call x1, Pallas kernels, spmm_backward(): pl.pallas_call(spmm_backward_kernel, out_shape=jax.ShapeDtypeStruct((col_...  15.8 us
    ppermute x1, starting transfers between devices, scatter_rows(): return mine + lax.ppermute(other, 'zh', [(0, 1), (1, 0)])  10.8 us
  transfers between devices with their start and end apart: 3, of which 3 were waited for; matrix products, arithmetic and copies ran while one was open for 0% of the time, Pallas kernels for 0%

profile of v2, /device:TPU:14, one launch (start us, length us, event | category | flops | bytes accessed | tf_op | source)
XLA Modules:
  0.0 252.1 jit_solution(18203166861719804668)
XLA Ops:
  0.6 16.1 %all_gather.6 = bf16[256,128]{1,0:T(8,128)(2,1)S(1)} all-gather(bf16[128,128]{1,0:T(8,128)(2,1)} %param.7), channel_id=1, replica_groups=mesh['y'=8,'x'=4,'zh'=2,'zl'=6,'core'=2] {'zh'}, dimensions={0}, use_global_device_ids=true | all-gather | bytes 98304 | tf_op jit(solution)/shard_map/all_gather | solution.py:110
  16.7 1.8 broadcast_in_dim.2
  18.5 10.1 %all-to-all-start = ((bf16[32,256,128]{2,1,0:T(8,128)(2,1)}), bf16[32,256,128]{2,1,0:T(8,128)(2,1)S(1)}, u32[]{:S(2)}, u32[]{:S(2)}) async-start(bf16[32,256,128]{2,1,0:T(8,128)(2,1)} %broadcast_in_dim.2), calls=%async_computation | async-start | bytes 4194304 | tf_op jit(solution)/shard_map/all_to_all | solution.py:113
  29.2 48.2 %all-to-all-done = bf16[32,256,128]{2,1,0:T(8,128)(2,1)S(1)} async-done(((bf16[32,256,128]{2,1,0:T(8,128)(2,1)}), bf16[32,256,128]{2,1,0:T(8,128)(2,1)S(1)}, u32[]{:S(2)}, u32[]{:S(2)}) %all-to-all-start) | async-done | bytes 2097184 | tf_op jit(solution)/shard_map/all_to_all | solution.py:113
  77.4 0.0 copy-start
  77.4 1.3 copy-done
  78.7 23.7 %shard_map.86 = bf16[1536,256]{1,0:T(8,128)(2,1)} custom-call(s32[72]{0:T(128)} %bitcast.24, s32[72]{0:T(128)} %bitcast.26, s32[1]{0:T(128)} %bitcast.15.count_ref, bf16[8192,128]{1,0:T(8,128)(2,1)} %bitcast.20, bf16[128,256]{1,0:T(8,128)(2,1)} %w_ref.1, bf16[72,128,128]{2,1,0:T(8,128)(2,1)} %bitcast.17), custom_call_target="tpu_custom_call" | custom-call | flops 1207959552 | bytes 5242880 | tf_op jit(solution)/shard_map/pallas_call | solution.py:75
  102.4 0.0 copy-start.1
  102.4 0.0 copy-start.2
  102.4 37.5 %all_to_all.15 = bf16[12,128,256]{2,1,0:T(8,128)(2,1)S(1)} all-to-all(bf16[12,128,256]{2,1,0:T(8,128)(2,1)} %bitcast.21), channel_id=1, replica_groups=mesh['y'=8,'x'=4,'zh'=2,'zl'=6,'core'=2] {'zl','core'}, dimensions={0} | all-to-all | bytes 1572864 | tf_op jit(solution)/shard_map/all_to_all | solution.py:141
  139.9 0.1 convert_reduce_fusion.1
  140.0 0.0 copy-done.1
  140.0 0.0 copy-done.2
  140.0 0.2 convolution_convert_fusion
  140.2 22.5 %all_gather.7.back_ref = bf16[1536,128]{1,0:T(8,128)(2,1)} all-gather(bf16[128,128]{1,0:T(8,128)(2,1)S(1)} %convolution_convert_fusion), channel_id=1, replica_groups=mesh['y'=8,'x'=4,'zh'=2,'zl'=6,'core'=2] {'zl','core'}, dimensions={0}, use_global_device_ids=true | all-gather | bytes 425984 | tf_op jit(solution)/shard_map/all_gather | solution.py:148
  162.7 15.8 %shard_map.87 = bf16[8192,128]{1,0:T(8,128)(2,1)} custom-call(s32[72]{0:T(128)} %bitcast.25, s32[72]{0:T(128)} %bitcast.27, s32[1]{0:T(128)} %bitcast.16.count_ref, bf16[1536,128]{1,0:T(8,128)(2,1)} %all_gather.7.back_ref, bf16[72,128,128]{2,1,0:T(8,128)(2,1)} %bitcast.18), custom_call_target="tpu_custom_call" | custom-call | flops 301989888 | bytes 4849664 | tf_op jit(solution)/shard_map/pallas_call | solution.py:94
  178.4 8.5 %all-to-all-start.2 = ((bf16[32,256,128]{2,1,0:T(8,128)(2,1)}), bf16[32,256,128]{2,1,0:T(8,128)(2,1)S(1)}, u32[]{:S(2)}, u32[]{:S(2)}) async-start(bf16[32,256,128]{2,1,0:T(8,128)(2,1)} %bitcast.19), calls=%async_computation.2 | async-start | bytes 4194304 | tf_op jit(solution)/shard_map/all_to_all | solution.py:119
  187.0 49.8 %all-to-all-done.2 = bf16[32,256,128]{2,1,0:T(8,128)(2,1)S(1)} async-done(((bf16[32,256,128]{2,1,0:T(8,128)(2,1)}), bf16[32,256,128]{2,1,0:T(8,128)(2,1)S(1)}, u32[]{:S(2)}, u32[]{:S(2)}) %all-to-all-start.2) | async-done | bytes 2097184 | tf_op jit(solution)/shard_map/all_to_all | solution.py:119
  236.8 0.3 convert_reduce_fusion
  237.1 10.8 %collective-permute-start = (f32[128,128]{1,0:T(8,128)S(1)}, f32[128,128]{1,0:T(8,128)S(1)}, u32[]{:S(2)}, u32[]{:S(2)}) collective-permute-start(f32[128,128]{1,0:T(8,128)S(1)} %dynamic-slice_bitcast_fusion), channel_id=1, source_target_pairs={{0,12},{12,0},{1,13},{13,1},{2,14},{14,2},{3,15},{15,3},{4,16},{16... | collective-permute-start | bytes 196616 | tf_op jit(solution)/shard_map/ppermute | solution.py:123
  247.8 0.7 multiply_convert_fusion.1
  248.5 3.0 %collective-permute-done = f32[128,128]{1,0:T(8,128)S(1)} collective-permute-done((f32[128,128]{1,0:T(8,128)S(1)}, f32[128,128]{1,0:T(8,128)S(1)}, u32[]{:S(2)}, u32[]{:S(2)}) %collective-permute-start) | collective-permute-done | bytes 65568 | tf_op jit(solution)/shard_map/ppermute | solution.py:123
  251.5 0.6 fusion
  (1 shorter events, 0.0 us)
Async XLA Ops:
  18.5 58.9 %all-to-all-start = ((bf16[32,256,128]{2,1,0:T(8,128)(2,1)}), bf16[32,256,128]{2,1,0:T(8,128)(2,1)S(1)}, u32[]{:S(2)}, u32[]{:S(2)}) async-start(bf16[32,256,128]{2,1,0:T(8,128)(2,1)} %broadcast_in_dim.2), calls=%async_computation | async-start | bytes 4194304 | tf_op jit(solution)/shard_map/all_to_all | solution.py:113
  77.4 1.3 copy-start
  102.4 37.6 %copy-start.1 = (bf16[128,256]{1,0:T(8,128)(2,1)S(1)}, bf16[128,256]{1,0:T(8,128)(2,1)}, u32[]{:S(2)}) copy-start(bf16[128,256]{1,0:T(8,128)(2,1)} %w_ref.1) | copy-start | bytes 196612
  102.4 37.6 %copy-start.2 = (bf16[128,256]{1,0:T(8,128)(2,1)S(1)}, bf16[128,256]{1,0:T(8,128)(2,1)}, u32[]{:S(2)}) copy-start(bf16[128,256]{1,0:T(8,128)(2,1)} %param.13) | copy-start | bytes 196612
  178.4 58.3 %all-to-all-start.2 = ((bf16[32,256,128]{2,1,0:T(8,128)(2,1)}), bf16[32,256,128]{2,1,0:T(8,128)(2,1)S(1)}, u32[]{:S(2)}, u32[]{:S(2)}) async-start(bf16[32,256,128]{2,1,0:T(8,128)(2,1)} %bitcast.19), calls=%async_computation.2 | async-start | bytes 4194304 | tf_op jit(solution)/shard_map/all_to_all | solution.py:119
  237.1 14.4 %collective-permute-start = (f32[128,128]{1,0:T(8,128)S(1)}, f32[128,128]{1,0:T(8,128)S(1)}, u32[]{:S(2)}, u32[]{:S(2)}) collective-permute-start(f32[128,128]{1,0:T(8,128)S(1)} %dynamic-slice_bitcast_fusion), channel_id=1, source_target_pairs={{0,12},{12,0},{1,13},{13,1},{2,14},{14,2},{3,15},{15,3},{4,16},{16... | collective-permute-start | bytes 196616 | tf_op jit(solution)/shard_map/ppermute | solution.py:123

commit v3 on v2

--- a/solution.py
+++ b/solution.py
@@ -13,27 +13,22 @@
 XY = ("y", "x")
 
 
-def spmm_forward_kernel(rows_ref, cols_ref, count_ref, feat_ref, w_ref, vals_ref, out_ref, acc_ref):
+def spmm_forward_kernel(rows_ref, cols_ref, count_ref, feat_ref, vals_ref, out_ref, acc_ref):
     block = vals_ref.shape[1]
     acc_ref[...] = jnp.zeros_like(acc_ref)
     last_row = acc_ref.shape[0] // block - 1
     last_col = feat_ref.shape[0] // block - 1
 
     def body(s, carry):
-        @pl.when(s < count_ref[0])
-        def _():
-            c = jnp.minimum(jnp.maximum(cols_ref[s], 0), last_col)
-            r = jnp.minimum(jnp.maximum(rows_ref[s], 0), last_row)
-            feat = feat_ref[pl.ds(pl.multiple_of(c * block, block), block), :]
-            source = jnp.dot(feat, w_ref[...], preferred_element_type=jnp.float32).astype(
-                jnp.bfloat16
-            )
-            rows = pl.ds(pl.multiple_of(r * block, block), block)
-            acc_ref[rows, :] += jnp.dot(vals_ref[s], source, preferred_element_type=jnp.float32)
-
+        c = jnp.minimum(jnp.maximum(cols_ref[s], 0), last_col)
+        r = jnp.minimum(jnp.maximum(rows_ref[s], 0), last_row)
+        feat = feat_ref[pl.ds(pl.multiple_of(c * block, block), block), :]
+        part = jnp.dot(vals_ref[s], feat, preferred_element_type=jnp.float32)
+        rows = pl.ds(pl.multiple_of(r * block, block), block)
+        acc_ref[rows, :] += jnp.where(s < count_ref[0], part, 0.0)
         return carry
 
-    lax.fori_loop(0, vals_ref.shape[0], body, 0)
+    lax.fori_loop(0, vals_ref.shape[0], body, 0, unroll=8)
     out_ref[...] = acc_ref[...].astype(out_ref.dtype)
 
 
@@ -44,20 +39,17 @@
     last_col = acc_ref.shape[0] // block - 1
 
     def body(s, carry):
-        @pl.when(s < count_ref[0])
-        def _():
-            c = jnp.minimum(jnp.maximum(cols_ref[s], 0), last_col)
-            r = jnp.minimum(jnp.maximum(rows_ref[s], 0), last_row)
-            source = back_ref[pl.ds(pl.multiple_of(r * block, block), block), :]
-            part = lax.dot_general(
-                vals_ref[s], source, (((0,), (0,)), ((), ())), preferred_element_type=jnp.float32
-            )
-            cols = pl.ds(pl.multiple_of(c * block, block), block)
-            acc_ref[cols, :] += part
-
+        c = jnp.minimum(jnp.maximum(cols_ref[s], 0), last_col)
+        r = jnp.minimum(jnp.maximum(rows_ref[s], 0), last_row)
+        source = back_ref[pl.ds(pl.multiple_of(r * block, block), block), :]
+        part = lax.dot_general(
+            vals_ref[s], source, (((0,), (0,)), ((), ())), preferred_element_type=jnp.float32
+        )
+        cols = pl.ds(pl.multiple_of(c * block, block), block)
+        acc_ref[cols, :] += jnp.where(s < count_ref[0], part, 0.0)
         return carry
 
-    lax.fori_loop(0, vals_ref.shape[0], body, 0)
+    lax.fori_loop(0, vals_ref.shape[0], body, 0, unroll=8)
     out_ref[...] = acc_ref[...].astype(out_ref.dtype)
 
 
@@ -67,24 +59,23 @@
     ] * n_vmem
 
 
-def spmm_forward(row_ids, col_ids, count, features, weight, values, row_blocks, interpret=False):
+def spmm_forward(row_ids, col_ids, count, features, values, row_blocks, interpret=False):
     block = values.shape[1]
-    width = weight.shape[1]
+    width = features.shape[1]
     slots = values.shape[0]
-    flops = slots * 2 * block * (features.shape[1] + block) * width
     return pl.pallas_call(
         spmm_forward_kernel,
         out_shape=jax.ShapeDtypeStruct((row_blocks * block, width), jnp.bfloat16),
-        in_specs=_specs(3, 3),
+        in_specs=_specs(3, 2),
         out_specs=pl.BlockSpec(memory_space=pltpu.VMEM),
         scratch_shapes=[pltpu.VMEM((row_blocks * block, width), jnp.float32)],
         cost_estimate=pl.CostEstimate(
-            flops=flops,
+            flops=slots * 2 * block * block * width,
             transcendentals=0,
             bytes_accessed=values.size * 2 + features.size * 2 + row_blocks * block * width * 2,
         ),
         interpret=interpret,
-    )(row_ids, col_ids, count, features, weight, values)
+    )(row_ids, col_ids, count, features, values)
 
 
 def spmm_backward(row_ids, col_ids, count, back, values, col_blocks, interpret=False):
@@ -136,9 +127,10 @@
 
     count = tile_count.reshape(1)
     features = gather_columns(node_features)
-    partial_value = spmm_forward(row_ids, col_ids, count, features, weight, values, row_blocks)
+    partial_value = spmm_forward(row_ids, col_ids, count, features, values, row_blocks)
     pieces = partial_value.reshape(n_col, node_rows, -1)
-    pre = lax.all_to_all(pieces, COL, 0, 0, tiled=False).astype(jnp.float32).sum(0)
+    aggregated = lax.all_to_all(pieces, COL, 0, 0, tiled=False).astype(jnp.float32).sum(0)
+    pre = jnp.dot(aggregated, weight.astype(jnp.float32), precision=lax.Precision.HIGHEST)
     sigm = jax.nn.sigmoid(pre)
     activations = (pre * sigm).astype(jnp.bfloat16)
     pre_grad = (grad_out.astype(jnp.float32) * (sigm * (1.0 + pre * (1.0 - sigm)))).astype(

time: 253 us -> 211 us (0.83)
  Pallas kernels: 39.5 us -> 11.4 us
  blocking collectives: 76 us -> 64.2 us
  starting transfers between devices: 29.4 us -> 26.7 us
    pallas_call x1, Pallas kernels: 23.7 us -> 5.3 us  [spmm_forward(): pl.pallas_call(spmm_forward_kernel, out_shape=jax.ShapeDtypeStruct((row_b...]
    all_to_all x1, blocking collectives: 37.5 us -> 25.3 us  [per_device(): lax.all_to_all(pieces, COL, 0, 0, tiled=False).astype(jnp.float32).sum(0)]
    pallas_call x1, Pallas kernels: 15.8 us -> 6.07 us  [spmm_backward(): pl.pallas_call(spmm_backward_kernel, out_shape=jax.ShapeDtypeStruct((col_...]
where the time goes in v3:
time: 211 us; the launch traced here: 210 us
  waiting for transfers between devices  101 us (48%)
  blocking collectives  64.2 us (30%)
  starting transfers between devices  26.7 us (13%)
  Pallas kernels  11.4 us (5%)
  local copies, waits for them, and re-layouts  3.16 us (1%)
    all_to_all x1, waiting for transfers between devices, scatter_rows(): lax.all_to_all(parts, XY, 0, 0, tiled=False).astype(jnp.float32).sum(0)  50.2 us
    all_to_all x1, waiting for transfers between devices, gather_columns(): return lax.all_to_all(spread, XY, 0, 0, tiled=False).reshape(-1, x.shape[1])  48.2 us
    all_to_all x1, blocking collectives, per_device(): lax.all_to_all(pieces, COL, 0, 0, tiled=False).astype(jnp.float32).sum(0)  25.3 us
    all_gather x1, blocking collectives, per_device(): rows_back = lax.all_gather(back, COL, axis=0, tiled=True)  22.7 us
    all_gather x1, blocking collectives, gather_columns(): pair = lax.all_gather(x, 'zh', axis=0, tiled=True)  16.2 us
    ppermute x1, starting transfers between devices, scatter_rows(): return mine + lax.ppermute(other, 'zh', [(0, 1), (1, 0)])  10.2 us
    all_to_all x1, starting transfers between devices, gather_columns(): return lax.all_to_all(spread, XY, 0, 0, tiled=False).reshape(-1, x.shape[1])  10.1 us
    all_to_all x1, starting transfers between devices, scatter_rows(): lax.all_to_all(parts, XY, 0, 0, tiled=False).astype(jnp.float32).sum(0)  6.43 us
  transfers between devices with their start and end apart: 3, of which 3 were waited for; matrix products, arithmetic and copies ran while one was open for 0% of the time, Pallas kernels for 0%

profile of v3, /device:TPU:14, one launch (start us, length us, event | category | flops | bytes accessed | tf_op | source)
XLA Modules:
  0.0 210.1 jit_solution(4953406418408466773)
XLA Ops:
  0.6 0.0 copy-start
  0.6 16.2 %all_gather.6 = bf16[256,128]{1,0:T(8,128)(2,1)S(1)} all-gather(bf16[128,128]{1,0:T(8,128)(2,1)} %param.7), channel_id=1, replica_groups=mesh['y'=8,'x'=4,'zh'=2,'zl'=6,'core'=2] {'zh'}, dimensions={0}, use_global_device_ids=true | all-gather | bytes 98304 | tf_op jit(solution)/shard_map/all_gather | solution.py:101
  16.8 1.8 broadcast_in_dim.2
  18.6 10.1 %all-to-all-start = ((bf16[32,256,128]{2,1,0:T(8,128)(2,1)}), bf16[32,256,128]{2,1,0:T(8,128)(2,1)S(1)}, u32[]{:S(2)}, u32[]{:S(2)}) async-start(bf16[32,256,128]{2,1,0:T(8,128)(2,1)} %broadcast_in_dim.2), calls=%async_computation | async-start | bytes 4194304 | tf_op jit(solution)/shard_map/all_to_all | solution.py:104
  29.4 48.2 %all-to-all-done = bf16[32,256,128]{2,1,0:T(8,128)(2,1)S(1)} async-done(((bf16[32,256,128]{2,1,0:T(8,128)(2,1)}), bf16[32,256,128]{2,1,0:T(8,128)(2,1)S(1)}, u32[]{:S(2)}, u32[]{:S(2)}) %all-to-all-start) | async-done | bytes 2097184 | tf_op jit(solution)/shard_map/all_to_all | solution.py:104
  77.5 0.0 copy-start.1
  77.5 1.3 copy-done.1
  78.9 0.0 copy-start.2
  78.9 5.3 %shard_map.86 = bf16[1536,128]{1,0:T(8,128)(2,1)} custom-call(s32[72]{0:T(128)} %bitcast.26, s32[72]{0:T(128)} %bitcast.28, s32[1]{0:T(128)} %bitcast.17.count_ref, bf16[8192,128]{1,0:T(8,128)(2,1)} %bitcast.22, bf16[72,128,128]{2,1,0:T(8,128)(2,1)} %bitcast.19), custom_call_target="tpu_custom_call" | custom-call | flops 301989888 | bytes 4849664 | tf_op jit(solution)/shard_map/pallas_call | solution.py:66
  84.2 25.3 %all_to_all.15 = bf16[12,128,128]{2,1,0:T(8,128)(2,1)S(1)} all-to-all(bf16[12,128,128]{2,1,0:T(8,128)(2,1)} %bitcast.23), channel_id=1, replica_groups=mesh['y'=8,'x'=4,'zh'=2,'zl'=6,'core'=2] {'zl','core'}, dimensions={0} | all-to-all | bytes 786432 | tf_op jit(solution)/shard_map/all_to_all | solution.py:132
  109.5 0.1 convert_reduce_fusion.1
  109.5 0.0 copy-done
  109.5 0.9 multiply_convert_fusion.1
  110.4 0.0 copy-done.2
  110.4 0.2 convolution_convert_fusion
  110.6 22.7 %all_gather.7.back_ref = bf16[1536,128]{1,0:T(8,128)(2,1)} all-gather(bf16[128,128]{1,0:T(8,128)(2,1)S(1)} %convolution_convert_fusion), channel_id=1, replica_groups=mesh['y'=8,'x'=4,'zh'=2,'zl'=6,'core'=2] {'zl','core'}, dimensions={0}, use_global_device_ids=true | all-gather | bytes 425984 | tf_op jit(solution)/shard_map/all_gather | solution.py:140
  133.3 6.1 %shard_map.87 = bf16[8192,128]{1,0:T(8,128)(2,1)} custom-call(s32[72]{0:T(128)} %bitcast.27, s32[72]{0:T(128)} %bitcast.29, s32[1]{0:T(128)} %bitcast.18.count_ref, bf16[1536,128]{1,0:T(8,128)(2,1)} %all_gather.7.back_ref, bf16[72,128,128]{2,1,0:T(8,128)(2,1)} %bitcast.20), custom_call_target="tpu_custom_call" | custom-call | flops 301989888 | bytes 4849664 | tf_op jit(solution)/shard_map/pallas_call | solution.py:85
  139.3 6.4 %all-to-all-start.2 = ((bf16[32,256,128]{2,1,0:T(8,128)(2,1)}), bf16[32,256,128]{2,1,0:T(8,128)(2,1)S(1)}, u32[]{:S(2)}, u32[]{:S(2)}) async-start(bf16[32,256,128]{2,1,0:T(8,128)(2,1)} %bitcast.21), calls=%async_computation.2 | async-start | bytes 4194304 | tf_op jit(solution)/shard_map/all_to_all | solution.py:110
  145.8 50.2 %all-to-all-done.2 = bf16[32,256,128]{2,1,0:T(8,128)(2,1)S(1)} async-done(((bf16[32,256,128]{2,1,0:T(8,128)(2,1)}), bf16[32,256,128]{2,1,0:T(8,128)(2,1)S(1)}, u32[]{:S(2)}, u32[]{:S(2)}) %all-to-all-start.2) | async-done | bytes 2097184 | tf_op jit(solution)/shard_map/all_to_all | solution.py:110
  195.9 0.3 convert_reduce_fusion
  196.3 10.2 %collective-permute-start = (f32[128,128]{1,0:T(8,128)S(1)}, f32[128,128]{1,0:T(8,128)S(1)}, u32[]{:S(2)}, u32[]{:S(2)}) collective-permute-start(f32[128,128]{1,0:T(8,128)S(1)} %dynamic-slice_bitcast_fusion), channel_id=1, source_target_pairs={{0,12},{12,0},{1,13},{13,1},{2,14},{14,2},{3,15},{15,3},{4,16},{16... | collective-permute-start | bytes 196616 | tf_op jit(solution)/shard_map/ppermute | solution.py:114
  206.5 3.0 %collective-permute-done = f32[128,128]{1,0:T(8,128)S(1)} collective-permute-done((f32[128,128]{1,0:T(8,128)S(1)}, f32[128,128]{1,0:T(8,128)S(1)}, u32[]{:S(2)}, u32[]{:S(2)}) %collective-permute-start) | collective-permute-done | bytes 65568 | tf_op jit(solution)/shard_map/ppermute | solution.py:114
  209.4 0.6 fusion
  (1 shorter events, 0.0 us)
Async XLA Ops:
  0.6 108.9 %copy-start = (bf16[128,256]{1,0:T(8,128)(2,1)S(1)}, bf16[128,256]{1,0:T(8,128)(2,1)}, u32[]{:S(2)}) copy-start(bf16[128,256]{1,0:T(8,128)(2,1)} %param.8) | copy-start | bytes 196612
  18.6 58.9 %all-to-all-start = ((bf16[32,256,128]{2,1,0:T(8,128)(2,1)}), bf16[32,256,128]{2,1,0:T(8,128)(2,1)S(1)}, u32[]{:S(2)}, u32[]{:S(2)}) async-start(bf16[32,256,128]{2,1,0:T(8,128)(2,1)} %broadcast_in_dim.2), calls=%async_computation | async-start | bytes 4194304 | tf_op jit(solution)/shard_map/all_to_all | solution.py:104
  77.5 1.3 copy-start.1
  78.9 31.5 %copy-start.2 = (bf16[128,256]{1,0:T(8,128)(2,1)S(1)}, bf16[128,256]{1,0:T(8,128)(2,1)}, u32[]{:S(2)}) copy-start(bf16[128,256]{1,0:T(8,128)(2,1)} %param.13) | copy-start | bytes 196612
  139.3 56.6 %all-to-all-start.2 = ((bf16[32,256,128]{2,1,0:T(8,128)(2,1)}), bf16[32,256,128]{2,1,0:T(8,128)(2,1)S(1)}, u32[]{:S(2)}, u32[]{:S(2)}) async-start(bf16[32,256,128]{2,1,0:T(8,128)(2,1)} %bitcast.21), calls=%async_computation.2 | async-start | bytes 4194304 | tf_op jit(solution)/shard_map/all_to_all | solution.py:110
  196.3 13.2 %collective-permute-start = (f32[128,128]{1,0:T(8,128)S(1)}, f32[128,128]{1,0:T(8,128)S(1)}, u32[]{:S(2)}, u32[]{:S(2)}) collective-permute-start(f32[128,128]{1,0:T(8,128)S(1)} %dynamic-slice_bitcast_fusion), channel_id=1, source_target_pairs={{0,12},{12,0},{1,13},{13,1},{2,14},{14,2},{3,15},{15,3},{4,16},{16... | collective-permute-start | bytes 196616 | tf_op jit(solution)/shard_map/ppermute | solution.py:114

commit v4 on v3

--- a/solution.py
+++ b/solution.py
@@ -28,7 +28,7 @@
         acc_ref[rows, :] += jnp.where(s < count_ref[0], part, 0.0)
         return carry
 
-    lax.fori_loop(0, vals_ref.shape[0], body, 0, unroll=8)
+    lax.fori_loop(0, vals_ref.shape[0], body, 0, unroll=True)
     out_ref[...] = acc_ref[...].astype(out_ref.dtype)
 
 
@@ -49,7 +49,7 @@
         acc_ref[cols, :] += jnp.where(s < count_ref[0], part, 0.0)
         return carry
 
-    lax.fori_loop(0, vals_ref.shape[0], body, 0, unroll=8)
+    lax.fori_loop(0, vals_ref.shape[0], body, 0, unroll=True)
     out_ref[...] = acc_ref[...].astype(out_ref.dtype)
 
 

time: 211 us -> 208 us (0.986)
  Pallas kernels: 11.4 us -> 8.53 us
where the time goes in v4:
time: 208 us; the launch traced here: 207 us
  waiting for transfers between devices  101 us (49%)
  blocking collectives  64.2 us (31%)
  starting transfers between devices  26.7 us (13%)
  Pallas kernels  8.53 us (4%)
  local copies, waits for them, and re-layouts  3.16 us (2%)
    all_to_all x1, waiting for transfers between devices, scatter_rows(): lax.all_to_all(parts, XY, 0, 0, tiled=False).astype(jnp.float32).sum(0)  50.2 us
    all_to_all x1, waiting for transfers between devices, gather_columns(): return lax.all_to_all(spread, XY, 0, 0, tiled=False).reshape(-1, x.shape[1])  48.2 us
    all_to_all x1, blocking collectives, per_device(): lax.all_to_all(pieces, COL, 0, 0, tiled=False).astype(jnp.float32).sum(0)  25.3 us
    all_gather x1, blocking collectives, per_device(): rows_back = lax.all_gather(back, COL, axis=0, tiled=True)  22.7 us
    all_gather x1, blocking collectives, gather_columns(): pair = lax.all_gather(x, 'zh', axis=0, tiled=True)  16.2 us
    ppermute x1, starting transfers between devices, scatter_rows(): return mine + lax.ppermute(other, 'zh', [(0, 1), (1, 0)])  10.2 us
    all_to_all x1, starting transfers between devices, gather_columns(): return lax.all_to_all(spread, XY, 0, 0, tiled=False).reshape(-1, x.shape[1])  10.1 us
    all_to_all x1, starting transfers between devices, scatter_rows(): lax.all_to_all(parts, XY, 0, 0, tiled=False).astype(jnp.float32).sum(0)  6.43 us
  transfers between devices with their start and end apart: 3, of which 3 were waited for; matrix products, arithmetic and copies ran while one was open for 0% of the time, Pallas kernels for 0%

profile of v4, /device:TPU:14, one launch (start us, length us, event | category | flops | bytes accessed | tf_op | source)
XLA Modules:
  0.0 207.2 jit_solution(5455057044199239875)
XLA Ops:
  0.6 0.0 copy-start
  0.6 16.2 %all_gather.6 = bf16[256,128]{1,0:T(8,128)(2,1)S(1)} all-gather(bf16[128,128]{1,0:T(8,128)(2,1)} %param.7), channel_id=1, replica_groups=mesh['y'=8,'x'=4,'zh'=2,'zl'=6,'core'=2] {'zh'}, dimensions={0}, use_global_device_ids=true | all-gather | bytes 98304 | tf_op jit(solution)/shard_map/all_gather | solution.py:101
  16.8 1.8 broadcast_in_dim.2
  18.6 10.1 %all-to-all-start = ((bf16[32,256,128]{2,1,0:T(8,128)(2,1)}), bf16[32,256,128]{2,1,0:T(8,128)(2,1)S(1)}, u32[]{:S(2)}, u32[]{:S(2)}) async-start(bf16[32,256,128]{2,1,0:T(8,128)(2,1)} %broadcast_in_dim.2), calls=%async_computation | async-start | bytes 4194304 | tf_op jit(solution)/shard_map/all_to_all | solution.py:104
  29.4 48.2 %all-to-all-done = bf16[32,256,128]{2,1,0:T(8,128)(2,1)S(1)} async-done(((bf16[32,256,128]{2,1,0:T(8,128)(2,1)}), bf16[32,256,128]{2,1,0:T(8,128)(2,1)S(1)}, u32[]{:S(2)}, u32[]{:S(2)}) %all-to-all-start) | async-done | bytes 2097184 | tf_op jit(solution)/shard_map/all_to_all | solution.py:104
  77.5 0.0 copy-start.1
  77.5 1.3 copy-done.1
  78.9 0.0 copy-start.2
  78.9 4.0 %shard_map.86 = bf16[1536,128]{1,0:T(8,128)(2,1)} custom-call(s32[72]{0:T(128)} %bitcast.26, s32[72]{0:T(128)} %bitcast.28, s32[1]{0:T(128)} %bitcast.17.count_ref, bf16[8192,128]{1,0:T(8,128)(2,1)} %bitcast.22, bf16[72,128,128]{2,1,0:T(8,128)(2,1)} %bitcast.19), custom_call_target="tpu_custom_call" | custom-call | flops 301989888 | bytes 4849664 | tf_op jit(solution)/shard_map/pallas_call | solution.py:66
  82.8 25.3 %all_to_all.15 = bf16[12,128,128]{2,1,0:T(8,128)(2,1)S(1)} all-to-all(bf16[12,128,128]{2,1,0:T(8,128)(2,1)} %bitcast.23), channel_id=1, replica_groups=mesh['y'=8,'x'=4,'zh'=2,'zl'=6,'core'=2] {'zl','core'}, dimensions={0} | all-to-all | bytes 786432 | tf_op jit(solution)/shard_map/all_to_all | solution.py:132
  108.1 0.1 convert_reduce_fusion.1
  108.2 0.0 copy-done
  108.2 0.9 multiply_convert_fusion.1
  109.1 0.0 copy-done.2
  109.1 0.2 convolution_convert_fusion
  109.2 22.7 %all_gather.7.back_ref = bf16[1536,128]{1,0:T(8,128)(2,1)} all-gather(bf16[128,128]{1,0:T(8,128)(2,1)S(1)} %convolution_convert_fusion), channel_id=1, replica_groups=mesh['y'=8,'x'=4,'zh'=2,'zl'=6,'core'=2] {'zl','core'}, dimensions={0}, use_global_device_ids=true | all-gather | bytes 425984 | tf_op jit(solution)/shard_map/all_gather | solution.py:140
  131.9 4.6 %shard_map.87 = bf16[8192,128]{1,0:T(8,128)(2,1)} custom-call(s32[72]{0:T(128)} %bitcast.27, s32[72]{0:T(128)} %bitcast.29, s32[1]{0:T(128)} %bitcast.18.count_ref, bf16[1536,128]{1,0:T(8,128)(2,1)} %all_gather.7.back_ref, bf16[72,128,128]{2,1,0:T(8,128)(2,1)} %bitcast.20), custom_call_target="tpu_custom_call" | custom-call | flops 301989888 | bytes 4849664 | tf_op jit(solution)/shard_map/pallas_call | solution.py:85
  136.5 6.4 %all-to-all-start.2 = ((bf16[32,256,128]{2,1,0:T(8,128)(2,1)}), bf16[32,256,128]{2,1,0:T(8,128)(2,1)S(1)}, u32[]{:S(2)}, u32[]{:S(2)}) async-start(bf16[32,256,128]{2,1,0:T(8,128)(2,1)} %bitcast.21), calls=%async_computation.2 | async-start | bytes 4194304 | tf_op jit(solution)/shard_map/all_to_all | solution.py:110
  142.9 50.2 %all-to-all-done.2 = bf16[32,256,128]{2,1,0:T(8,128)(2,1)S(1)} async-done(((bf16[32,256,128]{2,1,0:T(8,128)(2,1)}), bf16[32,256,128]{2,1,0:T(8,128)(2,1)S(1)}, u32[]{:S(2)}, u32[]{:S(2)}) %all-to-all-start.2) | async-done | bytes 2097184 | tf_op jit(solution)/shard_map/all_to_all | solution.py:110
  193.1 0.3 convert_reduce_fusion
  193.4 10.2 %collective-permute-start = (f32[128,128]{1,0:T(8,128)S(1)}, f32[128,128]{1,0:T(8,128)S(1)}, u32[]{:S(2)}, u32[]{:S(2)}) collective-permute-start(f32[128,128]{1,0:T(8,128)S(1)} %dynamic-slice_bitcast_fusion), channel_id=1, source_target_pairs={{0,12},{12,0},{1,13},{13,1},{2,14},{14,2},{3,15},{15,3},{4,16},{16... | collective-permute-start | bytes 196616 | tf_op jit(solution)/shard_map/ppermute | solution.py:114
  203.6 3.0 %collective-permute-done = f32[128,128]{1,0:T(8,128)S(1)} collective-permute-done((f32[128,128]{1,0:T(8,128)S(1)}, f32[128,128]{1,0:T(8,128)S(1)}, u32[]{:S(2)}, u32[]{:S(2)}) %collective-permute-start) | collective-permute-done | bytes 65568 | tf_op jit(solution)/shard_map/ppermute | solution.py:114
  206.6 0.6 fusion
  (1 shorter events, 0.0 us)
Async XLA Ops:
  0.6 107.6 %copy-start = (bf16[128,256]{1,0:T(8,128)(2,1)S(1)}, bf16[128,256]{1,0:T(8,128)(2,1)}, u32[]{:S(2)}) copy-start(bf16[128,256]{1,0:T(8,128)(2,1)} %param.8) | copy-start | bytes 196612
  18.6 58.9 %all-to-all-start = ((bf16[32,256,128]{2,1,0:T(8,128)(2,1)}), bf16[32,256,128]{2,1,0:T(8,128)(2,1)S(1)}, u32[]{:S(2)}, u32[]{:S(2)}) async-start(bf16[32,256,128]{2,1,0:T(8,128)(2,1)} %broadcast_in_dim.2), calls=%async_computation | async-start | bytes 4194304 | tf_op jit(solution)/shard_map/all_to_all | solution.py:104
  77.5 1.3 copy-start.1
  78.9 30.2 %copy-start.2 = (bf16[128,256]{1,0:T(8,128)(2,1)S(1)}, bf16[128,256]{1,0:T(8,128)(2,1)}, u32[]{:S(2)}) copy-start(bf16[128,256]{1,0:T(8,128)(2,1)} %param.13) | copy-start | bytes 196612
  136.5 56.6 %all-to-all-start.2 = ((bf16[32,256,128]{2,1,0:T(8,128)(2,1)}), bf16[32,256,128]{2,1,0:T(8,128)(2,1)S(1)}, u32[]{:S(2)}, u32[]{:S(2)}) async-start(bf16[32,256,128]{2,1,0:T(8,128)(2,1)} %bitcast.21), calls=%async_computation.2 | async-start | bytes 4194304 | tf_op jit(solution)/shard_map/all_to_all | solution.py:110
  193.4 13.2 %collective-permute-start = (f32[128,128]{1,0:T(8,128)S(1)}, f32[128,128]{1,0:T(8,128)S(1)}, u32[]{:S(2)}, u32[]{:S(2)}) collective-permute-start(f32[128,128]{1,0:T(8,128)S(1)} %dynamic-slice_bitcast_fusion), channel_id=1, source_target_pairs={{0,12},{12,0},{1,13},{13,1},{2,14},{14,2},{3,15},{15,3},{4,16},{16... | collective-permute-start | bytes 196616 | tf_op jit(solution)/shard_map/ppermute | solution.py:114

commit v5 on v4

--- a/solution.py
+++ b/solution.py
@@ -111,7 +111,8 @@
     halves = got.reshape(2, -1, total.shape[1])
     mine = lax.dynamic_index_in_dim(halves, zh, 0, keepdims=False)
     other = lax.dynamic_index_in_dim(halves, 1 - zh, 0, keepdims=False)
-    return mine + lax.ppermute(other, "zh", [(0, 1), (1, 0)])
+    swapped = lax.all_gather(other, "zh", axis=0, tiled=False)
+    return mine + lax.dynamic_index_in_dim(swapped, 1 - zh, 0, keepdims=False)
 
 
 def per_device(node_features, weight, block_values, tile_rows, tile_cols, tile_count, grad_out):

time: 208 us -> 206 us (level)
  blocking collectives: 64.2 us -> 76.1 us
  starting transfers between devices: 26.7 us -> 16.5 us
  waiting for transfers between devices: 101 us -> 98.3 us
    all_gather x0 -> x1, blocking collectives: none -> 12 us  [scatter_rows(): swapped = lax.all_gather(other, 'zh', axis=0, tiled=False)]
    ppermute x1 -> x0, starting transfers between devices: 10.2 us -> none  [scatter_rows(): return mine + lax.ppermute(other, 'zh', [(0, 1), (1, 0)])]
    ppermute x1 -> x0, waiting for transfers between devices: 2.96 us -> none  [scatter_rows(): return mine + lax.ppermute(other, 'zh', [(0, 1), (1, 0)])]
  transfers between devices with their start and end apart: 3 -> 2, of which waited for: 3 -> 2; matrix products, arithmetic and copies ran while one was open for 0% -> 0% of each run, Pallas kernels for 0% -> 0%
where the time goes in v5:
time: 206 us
  waiting for transfers between devices  98.3 us (48%)
  blocking collectives  76.1 us (37%)
  starting transfers between devices  16.5 us (8%)
  Pallas kernels  8.54 us (4%)
  local copies, waits for them, and re-layouts  3.17 us (2%)
    all_to_all x1, waiting for transfers between devices, scatter_rows(): lax.all_to_all(parts, XY, 0, 0, tiled=False).astype(jnp.float32).sum(0)  50.2 us
    all_to_all x1, waiting for transfers between devices, gather_columns(): return lax.all_to_all(spread, XY, 0, 0, tiled=False).reshape(-1, x.shape[1])  48.2 us
    all_to_all x1, blocking collectives, per_device(): lax.all_to_all(pieces, COL, 0, 0, tiled=False).astype(jnp.float32).sum(0)  25.3 us
    all_gather x1, blocking collectives, per_device(): rows_back = lax.all_gather(back, COL, axis=0, tiled=True)  22.7 us
    all_gather x1, blocking collectives, gather_columns(): pair = lax.all_gather(x, 'zh', axis=0, tiled=True)  16.2 us
    all_gather x1, blocking collectives, scatter_rows(): swapped = lax.all_gather(other, 'zh', axis=0, tiled=False)  12 us
    all_to_all x1, starting transfers between devices, gather_columns(): return lax.all_to_all(spread, XY, 0, 0, tiled=False).reshape(-1, x.shape[1])  10.1 us
    all_to_all x1, starting transfers between devices, scatter_rows(): lax.all_to_all(parts, XY, 0, 0, tiled=False).astype(jnp.float32).sum(0)  6.43 us
  transfers between devices with their start and end apart: 2, of which 2 were waited for; matrix products, arithmetic and copies ran while one was open for 0% of the time, Pallas kernels for 0%

profile of v5, /device:TPU:14, one launch (start us, length us, event | category | flops | bytes accessed | tf_op | source)
XLA Modules:
  0.0 206.0 jit_solution(8449240803465629857)
XLA Ops:
  0.6 0.0 copy-start
  0.6 16.2 %all_gather.10 = bf16[256,128]{1,0:T(8,128)(2,1)S(1)} all-gather(bf16[128,128]{1,0:T(8,128)(2,1)} %param.7), channel_id=1, replica_groups=mesh['y'=8,'x'=4,'zh'=2,'zl'=6,'core'=2] {'zh'}, dimensions={0}, use_global_device_ids=true | all-gather | bytes 98304 | tf_op jit(solution)/shard_map/all_gather | solution.py:101
  16.8 1.8 broadcast_in_dim.2
  18.6 10.1 %all-to-all-start = ((bf16[32,256,128]{2,1,0:T(8,128)(2,1)}), bf16[32,256,128]{2,1,0:T(8,128)(2,1)S(1)}, u32[]{:S(2)}, u32[]{:S(2)}) async-start(bf16[32,256,128]{2,1,0:T(8,128)(2,1)} %broadcast_in_dim.2), calls=%async_computation | async-start | bytes 4194304 | tf_op jit(solution)/shard_map/all_to_all | solution.py:104
  29.4 48.2 %all-to-all-done = bf16[32,256,128]{2,1,0:T(8,128)(2,1)S(1)} async-done(((bf16[32,256,128]{2,1,0:T(8,128)(2,1)}), bf16[32,256,128]{2,1,0:T(8,128)(2,1)S(1)}, u32[]{:S(2)}, u32[]{:S(2)}) %all-to-all-start) | async-done | bytes 2097184 | tf_op jit(solution)/shard_map/all_to_all | solution.py:104
  77.5 0.0 copy-start.1
  77.5 1.3 copy-done.1
  78.9 0.0 copy-start.2
  78.9 4.0 %shard_map.86 = bf16[1536,128]{1,0:T(8,128)(2,1)} custom-call(s32[72]{0:T(128)} %bitcast.22, s32[72]{0:T(128)} %bitcast.24, s32[1]{0:T(128)} %bitcast.13.count_ref, bf16[8192,128]{1,0:T(8,128)(2,1)} %bitcast.18, bf16[72,128,128]{2,1,0:T(8,128)(2,1)} %bitcast.15), custom_call_target="tpu_custom_call" | custom-call | flops 301989888 | bytes 4849664 | tf_op jit(solution)/shard_map/pallas_call | solution.py:66
  82.8 25.3 %all_to_all.15 = bf16[12,128,128]{2,1,0:T(8,128)(2,1)S(1)} all-to-all(bf16[12,128,128]{2,1,0:T(8,128)(2,1)} %bitcast.19), channel_id=1, replica_groups=mesh['y'=8,'x'=4,'zh'=2,'zl'=6,'core'=2] {'zl','core'}, dimensions={0} | all-to-all | bytes 786432 | tf_op jit(solution)/shard_map/all_to_all | solution.py:133
  108.1 0.1 convert_reduce_fusion.1
  108.2 0.0 copy-done
  108.2 0.9 multiply_convert_fusion.1
  109.1 0.0 copy-done.2
  109.1 0.2 convolution_convert_fusion
  109.2 22.7 %all_gather.11.back_ref = bf16[1536,128]{1,0:T(8,128)(2,1)} all-gather(bf16[128,128]{1,0:T(8,128)(2,1)S(1)} %convolution_convert_fusion), channel_id=1, replica_groups=mesh['y'=8,'x'=4,'zh'=2,'zl'=6,'core'=2] {'zl','core'}, dimensions={0}, use_global_device_ids=true | all-gather | bytes 425984 | tf_op jit(solution)/shard_map/all_gather | solution.py:141
  131.9 4.6 %shard_map.87 = bf16[8192,128]{1,0:T(8,128)(2,1)} custom-call(s32[72]{0:T(128)} %bitcast.23, s32[72]{0:T(128)} %bitcast.25, s32[1]{0:T(128)} %bitcast.14.count_ref, bf16[1536,128]{1,0:T(8,128)(2,1)} %all_gather.11.back_ref, bf16[72,128,128]{2,1,0:T(8,128)(2,1)} %bitcast.16), custom_call_target="tpu_custom_call" | custom-call | flops 301989888 | bytes 4849664 | tf_op jit(solution)/shard_map/pallas_call | solution.py:85
  136.5 6.4 %all-to-all-start.2 = ((bf16[32,256,128]{2,1,0:T(8,128)(2,1)}), bf16[32,256,128]{2,1,0:T(8,128)(2,1)S(1)}, u32[]{:S(2)}, u32[]{:S(2)}) async-start(bf16[32,256,128]{2,1,0:T(8,128)(2,1)} %bitcast.17), calls=%async_computation.2 | async-start | bytes 4194304 | tf_op jit(solution)/shard_map/all_to_all | solution.py:110
  142.9 50.2 %all-to-all-done.2 = bf16[32,256,128]{2,1,0:T(8,128)(2,1)S(1)} async-done(((bf16[32,256,128]{2,1,0:T(8,128)(2,1)}), bf16[32,256,128]{2,1,0:T(8,128)(2,1)S(1)}, u32[]{:S(2)}, u32[]{:S(2)}) %all-to-all-start.2) | async-done | bytes 2097184 | tf_op jit(solution)/shard_map/all_to_all | solution.py:110
  193.1 0.3 convert_reduce_fusion
  193.4 12.0 %all_gather.12 = f32[2,128,128]{2,1,0:T(8,128)S(1)} all-gather(f32[1,128,128]{2,1,0:T(8,128)S(1)} %constant_dynamic-slice_fusion), channel_id=1, replica_groups=mesh['y'=8,'x'=4,'zh'=2,'zl'=6,'core'=2] {'zh'}, dimensions={0}, use_global_device_ids=true | all-gather | bytes 196608 | tf_op jit(solution)/shard_map/all_gather | solution.py:114
  205.4 0.6 fusion
  (1 shorter events, 0.0 us)
Async XLA Ops:
  0.6 107.6 %copy-start = (bf16[128,256]{1,0:T(8,128)(2,1)S(1)}, bf16[128,256]{1,0:T(8,128)(2,1)}, u32[]{:S(2)}) copy-start(bf16[128,256]{1,0:T(8,128)(2,1)} %param.8) | copy-start | bytes 196612
  18.6 58.9 %all-to-all-start = ((bf16[32,256,128]{2,1,0:T(8,128)(2,1)}), bf16[32,256,128]{2,1,0:T(8,128)(2,1)S(1)}, u32[]{:S(2)}, u32[]{:S(2)}) async-start(bf16[32,256,128]{2,1,0:T(8,128)(2,1)} %broadcast_in_dim.2), calls=%async_computation | async-start | bytes 4194304 | tf_op jit(solution)/shard_map/all_to_all | solution.py:104
  77.5 1.3 copy-start.1
  78.9 30.2 %copy-start.2 = (bf16[128,256]{1,0:T(8,128)(2,1)S(1)}, bf16[128,256]{1,0:T(8,128)(2,1)}, u32[]{:S(2)}) copy-start(bf16[128,256]{1,0:T(8,128)(2,1)} %param.13) | copy-start | bytes 196612
  136.5 56.6 %all-to-all-start.2 = ((bf16[32,256,128]{2,1,0:T(8,128)(2,1)}), bf16[32,256,128]{2,1,0:T(8,128)(2,1)S(1)}, u32[]{:S(2)}, u32[]{:S(2)}) async-start(bf16[32,256,128]{2,1,0:T(8,128)(2,1)} %bitcast.17), calls=%async_computation.2 | async-start | bytes 4194304 | tf_op jit(solution)/shard_map/all_to_all | solution.py:110
